TPU v7x, 128 devices: a whole 4x4x4 slice. The times are simulated.
128 devices in a mesh: ctx: 8 (over x, y_hi), head: 16 (over y_lo, z, core).
Axes of the slice: x: 4, y: 4 (y_hi: 2, y_lo: 2; y = y_hi * 2 + y_lo), z: 4, core: 2. Of those that a mesh axis runs over, the one named last changes fastest.
Arguments:
- hidden_in: bfloat16 [8192, 5376], P(('ctx', 'head')), may hold values from -6 to 6
- pre_gain: float32 [5376], replicated, may hold values from 0.1 to 1.9
- w_query: bfloat16 [5376, 4096], P('ctx', 'head'), may hold values from -0.054554473 to 0.054554473, as said below
- w_key: bfloat16 [5376, 2048], P('ctx', 'head'), may hold values from -0.054554473 to 0.054554473, as said below
- value_weight: bfloat16 [5376, 2048], P('ctx', 'head'), may hold values from -0.078125 to 0.078125
- query_gain: float32 [128], replicated, may hold values from 0.6 to 7, as said below
- key_norm_gain: float32 [128], replicated, may hold values from 0.6 to 7, as said below
- w_output: bfloat16 [4096, 5376], P(('head', 'ctx')), may hold values from -0.09375 to 0.09375
- post_gain: float32 [5376], replicated, may hold values from 0.1 to 1.9
Outputs:
- layer_out: bfloat16 [8192, 5376], P(('ctx', 'head'))
Inputs may be any that keep to these rules, and one draw needn't show every extreme that they name: `w_query`: entries are normal draws clipped to 4 standard deviations, scaled by 5376 ** -0.5. `w_key`: entries are normal draws clipped to 4 standard deviations, scaled by 5376 ** -0.5. `query_gain`: positive gains. `key_norm_gain`: positive gains.
All inputs are finite; a program needn't handle non-finite values.
Results may differ from a plain program's by a relative error of at most 0.015.
The roundings to bfloat16 on the way count: a program that leaves them out, or rounds other values in their place, can miss the bound.
Values may be sent and summed in bfloat16 or wider, within the bound.
No kernel may reach another device: no remote copies, remote signals or barrier semaphores. Data moves between devices by JAX's collectives and lax.ppermute only.
A program may use at most 64 MiB of HBM per device.

v0:
```python
import jax
import jax.numpy as jnp
from jax import lax
from jax.sharding import Mesh, PartitionSpec as P

HEAD_SIZE = 128
WINDOW_SPAN = 1024
norm_eps = 1e-06
query_scale = 168.0 ** (-0.5)
rope_base = 10000.0
mask_value = -1e30
CTX = ("cx", "cy")
HEAD = ("hc", "core")


def passed_along(shard, axis, by):
    count = lax.axis_size(axis)
    pairs = [(i, i + by) for i in range(count) if 0 <= i + by < count]
    return lax.ppermute(shard, axis, pairs)


def rotated(shard, axis, by):
    count = lax.axis_size(axis)
    pairs = [(i, (i + by) % count) for i in range(count)]
    return lax.ppermute(shard, axis, pairs)


def placed(parts, me, count):
    stacked = jnp.zeros((count,) + parts[0].shape, parts[0].dtype)
    for i, part in enumerate(parts):
        stacked = lax.dynamic_update_index_in_dim(stacked, part, (me + i) % count, 0)
    return stacked


def ring_over_cx(piece):
    half = piece.shape[0] // 2
    from_left = rotated(piece, "cx", 1)
    from_right = rotated(piece, "cx", -1)
    far = jnp.concatenate(
        [rotated(from_left[:half], "cx", 1), rotated(from_right[half:], "cx", -1)]
    )
    return [piece, from_right, far, from_left]


def gathered_over_ctx(piece):
    cy = lax.axis_index("cy")
    cx = lax.axis_index("cx")
    own = ring_over_cx(piece)
    partner = ring_over_cx(rotated(piece, "cy", 1))
    pairs = [placed([a, b], cy, 2) for a, b in zip(own, partner)]
    ring = placed(pairs, cx, 4)
    return ring.reshape((8 * piece.shape[0],) + piece.shape[1:])


def root_mean_scale(values, scaling):
    mean_sq = jnp.mean(values * values, axis=-1, keepdims=True)
    return values * lax.rsqrt(mean_sq + norm_eps) * scaling


def apply_rotary(values, token_places):
    full_width = values.shape[-1]
    half_width = full_width // 2
    frequency = rope_base ** (-jnp.arange(half_width, dtype=jnp.float32) * 2.0 / full_width)
    angles = token_places.astype(jnp.float32)[:, None] * frequency[None, :]
    cosine = jnp.cos(angles)[:, None, :]
    sine_part = jnp.sin(angles)[:, None, :]
    lower_half = values[..., :half_width]
    upper_half = values[..., half_width:]
    return jnp.concatenate(
        [
            lower_half * cosine - upper_half * sine_part,
            upper_half * cosine + lower_half * sine_part,
        ],
        axis=-1,
    )


def body(
    hidden_in,
    pre_gain,
    w_query,
    w_key,
    value_weight,
    query_gain,
    key_norm_gain,
    w_output,
    post_gain,
):
    own_rows = hidden_in.astype(jnp.float32)
    q_cols = w_query.shape[1]
    k_cols = w_key.shape[1]
    w_in = gathered_over_ctx(jnp.concatenate([w_query, w_key, value_weight], axis=1))
    own_normed = root_mean_scale(own_rows, pre_gain).astype(jnp.bfloat16)
    normed = lax.all_gather(own_normed, HEAD, axis=0, tiled=True)
    normed, w_output = lax.optimization_barrier((normed, w_output))
    out_weight = gathered_over_ctx(w_output)
    tok_count = normed.shape[0]
    projected = jnp.dot(normed, w_in, preferred_element_type=jnp.float32)
    query_raw = projected[:, :q_cols]
    key_unnormed = projected[:, q_cols : q_cols + k_cols]
    value_unnormed = projected[:, q_cols + k_cols :]
    local_heads = q_cols // HEAD_SIZE
    local_groups = k_cols // HEAD_SIZE
    heads_per_group = local_heads // local_groups
    ctx_index = lax.axis_index(CTX)
    token_places = ctx_index * tok_count + jnp.arange(tok_count, dtype=jnp.int32)
    query_matrix = (
        apply_rotary(
            root_mean_scale(query_raw.reshape(tok_count, local_heads, HEAD_SIZE), query_gain),
            token_places,
        )
        * query_scale
    ).astype(jnp.bfloat16)
    projected_keys = apply_rotary(
        root_mean_scale(key_unnormed.reshape(tok_count, local_groups, HEAD_SIZE), key_norm_gain),
        token_places,
    ).astype(jnp.bfloat16)
    projected_values = value_unnormed.astype(jnp.bfloat16)
    key_value = jnp.stack(
        [projected_keys.reshape(tok_count, local_groups * HEAD_SIZE), projected_values]
    )
    pieces = [passed_along(key_value, CTX, 1)]
    extended = jnp.concatenate(pieces + [key_value], axis=1)
    band_keys = extended[0].reshape(-1, local_groups, HEAD_SIZE)
    band_values = extended[1].reshape(-1, local_groups, HEAD_SIZE)
    block_rows = min(512, tok_count)
    grouped_queries = query_matrix.reshape(tok_count, local_groups, heads_per_group, HEAD_SIZE)
    outputs = []
    for block_index in range(tok_count // block_rows):
        first_row = block_index * block_rows
        query_block = grouped_queries[first_row : first_row + block_rows]
        key_block = band_keys[first_row : first_row + block_rows + WINDOW_SPAN]
        value_block = band_values[first_row : first_row + block_rows + WINDOW_SPAN]
        scores = jnp.einsum(
            "qjgd,kjd->jgqk", query_block, key_block, preferred_element_type=jnp.float32
        )
        query_spots = token_places[first_row : first_row + block_rows]
        key_spots = (
            ctx_index * tok_count
            - WINDOW_SPAN
            + first_row
            + jnp.arange(block_rows + WINDOW_SPAN, dtype=jnp.int32)
        )
        allowed = (
            (key_spots[None, :] <= query_spots[:, None])
            & (key_spots[None, :] > query_spots[:, None] - WINDOW_SPAN)
            & (key_spots[None, :] >= 0)
        )
        scores = jnp.where(allowed, scores, mask_value)
        row_max = jnp.max(scores, axis=-1, keepdims=True)
        weights = jnp.exp(scores - row_max)
        row_sum = jnp.sum(weights, axis=-1, keepdims=True)
        probabilities = (weights / row_sum).astype(jnp.bfloat16)
        mixed = jnp.einsum(
            "jgqk,kjd->qjgd", probabilities, value_block, preferred_element_type=jnp.float32
        )
        outputs.append(mixed.astype(jnp.bfloat16).reshape(block_rows, local_heads * HEAD_SIZE))
    attended = jnp.concatenate(outputs, axis=0)
    partial_value = jnp.dot(attended, out_weight, preferred_element_type=jnp.float32).astype(
        jnp.bfloat16
    )
    summed = lax.psum_scatter(partial_value, HEAD, scatter_dimension=0, tiled=True).astype(
        jnp.float32
    )
    result = own_rows + root_mean_scale(summed, post_gain)
    return result.astype(jnp.bfloat16)


def solution(mesh):
    ctx_size, head_size = mesh.devices.shape
    view = Mesh(mesh.devices.reshape(ctx_size // 2, 2, head_size // 2, 2), CTX + HEAD)
    rows_spec = P(CTX + HEAD, None)
    cols_spec = P(CTX, HEAD)
    return jax.shard_map(
        body,
        mesh=view,
        in_specs=(
            rows_spec,
            P(),
            cols_spec,
            cols_spec,
            cols_spec,
            P(),
            P(),
            P(HEAD + CTX, None),
            P(),
        ),
        out_specs=rows_spec,
        check_vma=False,
    )
```

profile of v0, /device:TPU:0, one launch (start us, length us, event | category | flops | bytes accessed | tf_op | source)
XLA Modules:
  0.0 240.7 jit_solution(18410239072865604457)
XLA Ops:
  6.5 1.4 fusion.10
  8.0 2.2 fusion.12
  10.2 0.8 constant_dynamic-update-slice_fusion.2
  11.0 0.7 constant_dynamic-update-slice_fusion.1
  11.7 0.7 constant_dynamic-update-slice_fusion
  12.4 3.3 %collective-permute-start = (bf16[672,512]{1,0:T(8,128)(2,1)}, bf16[672,512]{1,0:T(8,128)(2,1)}, u32[]{:S(2)}, u32[]{:S(2)}) collective-permute-start(bf16[672,512]{1,0:T(8,128)(2,1)} %constant_dynamic-update-slice_fusion), channel_id=1, source_target_pairs={{0,16},{16,0},{1,17},{17,1},{2,18},{18,2},{3,19},{19,3},{4,20},{20... | collective-permute-start | bytes 2064392 | tf_op jit(solution)/shard_map/ppermute | solution.py:25
  15.7 2.8 %collective-permute-start.1 = (bf16[672,512]{1,0:T(8,128)(2,1)}, bf16[672,512]{1,0:T(8,128)(2,1)}, u32[]{:S(2)}, u32[]{:S(2)}) collective-permute-start(bf16[672,512]{1,0:T(8,128)(2,1)} %constant_dynamic-update-slice_fusion), channel_id=1, source_target_pairs={{0,96},{32,0},{64,32},{96,64},{1,97},{33,1},{65,33},{97,65},{2,98}... | collective-permute-start | bytes 2064392 | tf_op jit(solution)/shard_map/ppermute | solution.py:25
  18.7 1.2 bitcast_dynamic-update-slice_fusion.5
  19.8 1.1 and_and_fusion.1
  21.0 2.9 %multiply_cosine_fusion = (f32[1024,64]{1,0:T(8,128)S(1)}, f32[1024,64]{1,0:T(8,128)}) fusion(f32[64]{0:T(128)S(1)} %multiply_power_fusion, f32[1024]{0:T(1024)S(1)} %get-tuple-element.24), kind=kLoop, calls=%fused_computation.38 | loop fusion | flops 65536 | bytes 528640 | tf_op jit(solution)/shard_map/cos | solution.py:65
  23.9 1.1 and_and_fusion
  25.0 11.5 %collective-permute-done.3 = bf16[672,512]{1,0:T(8,128)(2,1)S(1)} collective-permute-done((bf16[672,512]{1,0:T(8,128)(2,1)}, bf16[672,512]{1,0:T(8,128)(2,1)S(1)}, u32[]{:S(2)}, u32[]{:S(2)}) %collective-permute-start.3) | collective-permute-done | bytes 688160 | tf_op jit(solution)/shard_map/ppermute | solution.py:25
  36.6 1.0 slice.106
  37.7 3.3 %collective-permute-start.5 = (bf16[336,512]{1,0:T(8,128)(2,1)S(1)}, bf16[336,512]{1,0:T(8,128)(2,1)S(1)}, u32[]{:S(2)}, u32[]{:S(2)}) collective-permute-start(bf16[336,512]{1,0:T(8,128)(2,1)S(1)} %slice.106), channel_id=1, source_target_pairs={{0,96},{32,0},{64,32},{96,64},{1,97},{33,1},{65,33},{97,65},{2,98}... | collective-permute-start | bytes 1032200 | tf_op jit(solution)/shard_map/ppermute | solution.py:25
  40.9 2.4 %collective-permute-start.2 = (bf16[672,512]{1,0:T(8,128)(2,1)}, bf16[672,512]{1,0:T(8,128)(2,1)S(1)}, u32[]{:S(2)}, u32[]{:S(2)}) collective-permute-start(bf16[672,512]{1,0:T(8,128)(2,1)} %collective-permute-done), channel_id=1, source_target_pairs={{0,96},{32,0},{64,32},{96,64},{1,97},{33,1},{65,33},{97,65},{2,98}... | collective-permute-start | bytes 2064392 | tf_op jit(solution)/shard_map/ppermute | solution.py:25
  43.5 1.2 bitcast_dynamic-update-slice_fusion.3
  44.6 1.2 bitcast_dynamic-update-slice_fusion.4
  45.8 2.8 %broadcast_in_dim.112 = bf16[4,2,672,512]{3,2,1,0:T(8,128)(2,1)} broadcast(bf16[]{:T(256)} %constant.186.clone.1), dimensions={} | broadcast | bytes 5505026 | tf_op jit(solution)/shard_map/broadcast_in_dim | solution.py:29
  48.6 1.2 constant_dynamic-update-slice_fusion.10
  50.1 10.9 %collective-permute-done.6 = bf16[672,512]{1,0:T(8,128)(2,1)S(1)} collective-permute-done((bf16[672,512]{1,0:T(8,128)(2,1)}, bf16[672,512]{1,0:T(8,128)(2,1)S(1)}, u32[]{:S(2)}, u32[]{:S(2)}) %collective-permute-start.6) | collective-permute-done | bytes 688160 | tf_op jit(solution)/shard_map/ppermute | solution.py:25
  61.2 0.3 collective-permute-done.2
  61.6 3.7 %collective-permute-start.8 = (bf16[336,512]{1,0:T(8,128)(2,1)S(1)}, bf16[336,512]{1,0:T(8,128)(2,1)S(1)}, u32[]{:S(2)}, u32[]{:S(2)}) collective-permute-start(bf16[336,512]{1,0:T(8,128)(2,1)S(1)} %slice.108), channel_id=1, source_target_pairs={{0,96},{32,0},{64,32},{96,64},{1,97},{33,1},{65,33},{97,65},{2,98}... | collective-permute-start | bytes 1032200 | tf_op jit(solution)/shard_map/ppermute | solution.py:25
  65.3 1.3 constant_dynamic-update-slice_fusion.9
  66.6 3.4 %collective-permute-done.7 = bf16[336,512]{1,0:T(8,128)(2,1)S(1)} collective-permute-done((bf16[336,512]{1,0:T(8,128)(2,1)S(1)}, bf16[336,512]{1,0:T(8,128)(2,1)S(1)}, u32[]{:S(2)}, u32[]{:S(2)}) %collective-permute-start.7) | collective-permute-done | bytes 344096 | tf_op jit(solution)/shard_map/ppermute | solution.py:25
  70.1 1.2 constant_dynamic-update-slice_fusion.8
  71.3 1.2 constant_dynamic-update-slice_fusion.7
  72.5 12.5 %all-gather.2.cloned.1.call-done = bf16[1024,5376]{1,0:T(8,128)(2,1)} async-done(((bf16[64,5376]{1,0:T(8,128)(2,1)}), bf16[1024,5376]{1,0:T(8,128)(2,1)}) %all-gather.2.cloned.1.call-update) | async-done | bytes 11010064 | tf_op jit(solution)/shard_map/all_gather | solution.py:94
  85.0 10.3 %fusion.48 = f32[1024,512]{0,1:T(8,128)S(1)} fusion(bf16[1024,5376]{1,0:T(8,128)(2,1)} %all-gather.2.cloned.1.call-done, bf16[5376,512]{1,0:T(8,128)(2,1)} %bitcast.8), kind=kOutput, calls=%fused_computation.115 | convolution fusion | flops 5637144576 | bytes 18612224 | tf_op jit(solution)/shard_map/dot_general | solution.py:98
  95.4 1.1 slice.115
  96.6 1.9 collective-permute-start.10
  98.6 2.8 %collective-permute-start.11 = (bf16[32,5376]{1,0:T(8,128)(2,1)}, bf16[32,5376]{1,0:T(8,128)(2,1)}, u32[]{:S(2)}, u32[]{:S(2)}) collective-permute-start(bf16[32,5376]{1,0:T(8,128)(2,1)} %param.16), channel_id=1, source_target_pairs={{0,96},{32,0},{64,32},{96,64},{1,97},{33,1},{65,33},{97,65},{2,98}... | collective-permute-start | bytes 1032200 | tf_op jit(solution)/shard_map/ppermute | solution.py:25
  101.4 1.2 fusion.42
  102.6 0.8 pad_maximum_fusion
  103.5 4.4 %collective-permute-start.9 = (bf16[2,1024,128]{1,2,0:T(8,128)(2,1)}, bf16[2,1024,128]{1,2,0:T(8,128)(2,1)}, u32[]{:S(2)}, u32[]{:S(2)}) collective-permute-start(bf16[2,1024,128]{1,2,0:T(8,128)(2,1)} %pad_maximum_fusion), channel_id=1, source_target_pairs={{0,16},{16,32},{32,48},{48,64},{64,80},{80,96},{96,112},{1,17},{17... | collective-permute-start | bytes 1572872 | tf_op jit(solution)/shard_map/ppermute | solution.py:19
  107.9 1.5 copy.10
  109.5 1.1 bitcast_dynamic-update-slice_fusion.11
  110.6 0.3 multiply_multiply_fusion
  110.9 0.5 multiply_subtract_fusion
  111.4 0.3 fusion.20
  111.8 0.7 collective-permute-done.13
  112.5 0.9 slice.122
  113.5 0.9 slice.123
  114.4 3.3 %collective-permute-start.15 = (bf16[16,5376]{1,0:T(8,128)(2,1)S(1)}, bf16[16,5376]{1,0:T(8,128)(2,1)S(1)}, u32[]{:S(2)}, u32[]{:S(2)}) collective-permute-start(bf16[16,5376]{1,0:T(8,128)(2,1)S(1)} %slice.123), channel_id=1, source_target_pairs={{0,96},{32,0},{64,32},{96,64},{1,97},{33,1},{65,33},{97,65},{2,98}... | collective-permute-start | bytes 516104 | tf_op jit(solution)/shard_map/ppermute | solution.py:25
  117.7 0.5 collective-permute-start.12
  118.3 1.5 collective-permute-start.16
  119.8 1.0 bitcast_dynamic-update-slice_fusion.10
  120.8 1.0 bitcast_dynamic-update-slice_fusion.9
  121.9 1.0 bitcast_dynamic-update-slice_fusion.7
  123.3 0.5 copy-done.3
  123.8 1.1 maximum_maximum_fusion
  124.9 1.3 fusion
  126.2 1.3 fusion.2
  127.5 2.0 fusion.14
  129.6 1.3 fusion.1
  130.9 1.3 fusion.3
  132.2 2.0 fusion.17
  134.2 1.2 collective-permute-start.17
  135.5 2.4 %collective-permute-start.18 = (bf16[16,5376]{1,0:T(8,128)(2,1)S(1)}, bf16[16,5376]{1,0:T(8,128)(2,1)S(1)}, u32[]{:S(2)}, u32[]{:S(2)}) collective-permute-start(bf16[16,5376]{1,0:T(8,128)(2,1)S(1)} %slice.125), channel_id=1, source_target_pairs={{0,96},{32,0},{64,32},{96,64},{1,97},{33,1},{65,33},{97,65},{2,98}... | collective-permute-start | bytes 516104 | tf_op jit(solution)/shard_map/ppermute | solution.py:25
  138.0 2.9 %collective-permute-done.17 = bf16[16,5376]{1,0:T(8,128)(2,1)S(1)} collective-permute-done((bf16[16,5376]{1,0:T(8,128)(2,1)S(1)}, bf16[16,5376]{1,0:T(8,128)(2,1)S(1)}, u32[]{:S(2)}, u32[]{:S(2)}) %collective-permute-start.17) | collective-permute-done | bytes 172064 | tf_op jit(solution)/shard_map/ppermute | solution.py:25
  140.9 0.3 collective-permute-done.18
  141.3 5.9 %convolution_convert_fusion = bf16[1024,5376]{1,0:T(8,128)(2,1)} fusion(bf16[256,5376]{1,0:T(8,128)(2,1)S(1)} %bitcast.131, bf16[512,256]{0,1:T(8,128)(2,1)S(1)} %bitcast.134, bf16[512,256]{0,1:T(8,128)(2,1)S(1)} %bitcast.133), kind=kOutput, calls=%fused_computation | convolution fusion | flops 2825125888 | bytes 14286848 | tf_op jit(solution)/shard_map/dot_general | solution.py:159
  147.2 83.0 %reduce-scatter.2.cloned.1.call-done = bf16[64,5376]{1,0:T(8,128)(2,1)} async-done(((bf16[1024,5376]{1,0:T(8,128)(2,1)}), bf16[64,5376]{1,0:T(8,128)(2,1)}) %reduce-scatter.2.cloned.1.call-update) | async-done | bytes 688144 | tf_op jit(solution)/shard_map/reduce_scatter | solution.py:162
  230.3 1.3 fusion.8
  231.6 2.3 fusion.13
  (82 shorter events, 2.2 us)
Async XLA Ops:
  6.5 3.7 %copy-start.4 = (bf16[672,256]{1,0:T(8,128)(2,1)S(1)}, bf16[672,256]{1,0:T(8,128)(2,1)}, u32[]{:S(2)}) copy-start(bf16[672,256]{1,0:T(8,128)(2,1)} %param.11) | copy-start | bytes 1032196
  6.5 4.5 %copy-start.5 = (bf16[672,128]{1,0:T(8,128)(2,1)S(1)}, bf16[672,128]{1,0:T(8,128)(2,1)}, u32[]{:S(2)}) copy-start(bf16[672,128]{1,0:T(8,128)(2,1)} %param.12) | copy-start | bytes 516100
  6.5 5.2 %copy-start.6 = (bf16[672,128]{1,0:T(8,128)(2,1)S(1)}, bf16[672,128]{1,0:T(8,128)(2,1)}, u32[]{:S(2)}) copy-start(bf16[672,128]{1,0:T(8,128)(2,1)} %param.13) | copy-start | bytes 516100
  6.5 78.5 %all-gather.2.cloned.1.call-start = ((), (), s32[]{:S(2)}) async-start(), calls=%async_computation.1 | async-start | bytes 11698176 | tf_op jit(solution)/shard_map/all_gather | solution.py:94
  10.2 220.1 %reduce-scatter.2.cloned.1.call-start = ((), (), s32[]{:S(2)}) async-start(), calls=%async_computation.2 | async-start | bytes 11698176 | tf_op jit(solution)/shard_map/reduce_scatter | solution.py:162
  12.4 28.5 %collective-permute-start = (bf16[672,512]{1,0:T(8,128)(2,1)}, bf16[672,512]{1,0:T(8,128)(2,1)}, u32[]{:S(2)}, u32[]{:S(2)}) collective-permute-start(bf16[672,512]{1,0:T(8,128)(2,1)} %constant_dynamic-update-slice_fusion), channel_id=1, source_target_pairs={{0,16},{16,0},{1,17},{17,1},{2,18},{18,2},{3,19},{19,3},{4,20},{20... | collective-permute-start | bytes 2064392 | tf_op jit(solution)/shard_map/ppermute | solution.py:25
  15.7 20.9 %collective-permute-start.1 = (bf16[672,512]{1,0:T(8,128)(2,1)}, bf16[672,512]{1,0:T(8,128)(2,1)}, u32[]{:S(2)}, u32[]{:S(2)}) collective-permute-start(bf16[672,512]{1,0:T(8,128)(2,1)} %constant_dynamic-update-slice_fusion), channel_id=1, source_target_pairs={{0,96},{32,0},{64,32},{96,64},{1,97},{33,1},{65,33},{97,65},{2,98}... | collective-permute-start | bytes 2064392 | tf_op jit(solution)/shard_map/ppermute | solution.py:25
  18.5 18.0 %collective-permute-start.3 = (bf16[672,512]{1,0:T(8,128)(2,1)}, bf16[672,512]{1,0:T(8,128)(2,1)S(1)}, u32[]{:S(2)}, u32[]{:S(2)}) collective-permute-start(bf16[672,512]{1,0:T(8,128)(2,1)} %constant_dynamic-update-slice_fusion), channel_id=1, source_target_pairs={{0,32},{32,64},{64,96},{96,0},{1,33},{33,65},{65,97},{97,1},{2,34}... | collective-permute-start | bytes 2064392 | tf_op jit(solution)/shard_map/ppermute | solution.py:25
  36.6 13.4 %collective-permute-start.4 = (bf16[336,512]{1,0:T(8,128)(2,1)S(1)}, bf16[336,512]{1,0:T(8,128)(2,1)S(1)}, u32[]{:S(2)}, u32[]{:S(2)}) collective-permute-start(bf16[336,512]{1,0:T(8,128)(2,1)S(1)} %slice.105), channel_id=1, source_target_pairs={{0,32},{32,64},{64,96},{96,0},{1,33},{33,65},{65,97},{97,1},{2,34}... | collective-permute-start | bytes 1032200 | tf_op jit(solution)/shard_map/ppermute | solution.py:25
  37.7 12.3 %collective-permute-start.5 = (bf16[336,512]{1,0:T(8,128)(2,1)S(1)}, bf16[336,512]{1,0:T(8,128)(2,1)S(1)}, u32[]{:S(2)}, u32[]{:S(2)}) collective-permute-start(bf16[336,512]{1,0:T(8,128)(2,1)S(1)} %slice.106), channel_id=1, source_target_pairs={{0,96},{32,0},{64,32},{96,64},{1,97},{33,1},{65,33},{97,65},{2,98}... | collective-permute-start | bytes 1032200 | tf_op jit(solution)/shard_map/ppermute | solution.py:25
  40.9 20.6 %collective-permute-start.2 = (bf16[672,512]{1,0:T(8,128)(2,1)}, bf16[672,512]{1,0:T(8,128)(2,1)S(1)}, u32[]{:S(2)}, u32[]{:S(2)}) collective-permute-start(bf16[672,512]{1,0:T(8,128)(2,1)} %collective-permute-done), channel_id=1, source_target_pairs={{0,96},{32,0},{64,32},{96,64},{1,97},{33,1},{65,33},{97,65},{2,98}... | collective-permute-start | bytes 2064392 | tf_op jit(solution)/shard_map/ppermute | solution.py:25
  43.4 17.7 %collective-permute-start.6 = (bf16[672,512]{1,0:T(8,128)(2,1)}, bf16[672,512]{1,0:T(8,128)(2,1)S(1)}, u32[]{:S(2)}, u32[]{:S(2)}) collective-permute-start(bf16[672,512]{1,0:T(8,128)(2,1)} %collective-permute-done), channel_id=1, source_target_pairs={{0,32},{32,64},{64,96},{96,0},{1,33},{33,65},{65,97},{97,1},{2,34}... | collective-permute-start | bytes 2064392 | tf_op jit(solution)/shard_map/ppermute | solution.py:25
  61.1 8.9 %collective-permute-start.7 = (bf16[336,512]{1,0:T(8,128)(2,1)S(1)}, bf16[336,512]{1,0:T(8,128)(2,1)S(1)}, u32[]{:S(2)}, u32[]{:S(2)}) collective-permute-start(bf16[336,512]{1,0:T(8,128)(2,1)S(1)} %slice.107), channel_id=1, source_target_pairs={{0,32},{32,64},{64,96},{96,0},{1,33},{33,65},{65,97},{97,1},{2,34}... | collective-permute-start | bytes 1032200 | tf_op jit(solution)/shard_map/ppermute | solution.py:25
  61.6 8.5 %collective-permute-start.8 = (bf16[336,512]{1,0:T(8,128)(2,1)S(1)}, bf16[336,512]{1,0:T(8,128)(2,1)S(1)}, u32[]{:S(2)}, u32[]{:S(2)}) collective-permute-start(bf16[336,512]{1,0:T(8,128)(2,1)S(1)} %slice.108), channel_id=1, source_target_pairs={{0,96},{32,0},{64,32},{96,64},{1,97},{33,1},{65,33},{97,65},{2,98}... | collective-permute-start | bytes 1032200 | tf_op jit(solution)/shard_map/ppermute | solution.py:25
  95.3 6.0 %copy-start.8 = (f32[128]{0:T(128)S(1)}, f32[128]{0:T(128)}, u32[]{:S(2)}) copy-start(f32[128]{0:T(128)} %param.15) | copy-start | bytes 1540
  96.6 21.1 %collective-permute-start.10 = (bf16[32,5376]{1,0:T(8,128)(2,1)}, bf16[32,5376]{1,0:T(8,128)(2,1)}, u32[]{:S(2)}, u32[]{:S(2)}) collective-permute-start(bf16[32,5376]{1,0:T(8,128)(2,1)} %param.16), channel_id=1, source_target_pairs={{0,16},{16,0},{1,17},{17,1},{2,18},{18,2},{3,19},{19,3},{4,20},{20... | collective-permute-start | bytes 1032200 | tf_op jit(solution)/shard_map/ppermute | solution.py:25
  98.6 14.9 %collective-permute-start.11 = (bf16[32,5376]{1,0:T(8,128)(2,1)}, bf16[32,5376]{1,0:T(8,128)(2,1)}, u32[]{:S(2)}, u32[]{:S(2)}) collective-permute-start(bf16[32,5376]{1,0:T(8,128)(2,1)} %param.16), channel_id=1, source_target_pairs={{0,96},{32,0},{64,32},{96,64},{1,97},{33,1},{65,33},{97,65},{2,98}... | collective-permute-start | bytes 1032200 | tf_op jit(solution)/shard_map/ppermute | solution.py:25
  101.3 11.2 %collective-permute-start.13 = (bf16[32,5376]{1,0:T(8,128)(2,1)}, bf16[32,5376]{1,0:T(8,128)(2,1)}, u32[]{:S(2)}, u32[]{:S(2)}) collective-permute-start(bf16[32,5376]{1,0:T(8,128)(2,1)} %param.16), channel_id=1, source_target_pairs={{0,32},{32,64},{64,96},{96,0},{1,33},{33,65},{65,97},{97,1},{2,34}... | collective-permute-start | bytes 1032200 | tf_op jit(solution)/shard_map/ppermute | solution.py:25
  101.4 9.1 %copy-start.9 = (f32[128]{0:T(128)S(1)}, f32[128]{0:T(128)}, u32[]{:S(2)}) copy-start(f32[128]{0:T(128)} %param.14) | copy-start | bytes 1540
  102.6 5.3 %copy-start.2 = (bf16[1,1024,64]{1,2,0:T(8,128)(2,1)}, bf16[1,1024,64]{1,2,0:T(8,128)(2,1)S(1)}, u32[]{:S(2)}) copy-start(bf16[1,1024,64]{1,2,0:T(8,128)(2,1)S(1)} %get-tuple-element.12) | copy-start | bytes 393220
  103.5 19.8 %collective-permute-start.9 = (bf16[2,1024,128]{1,2,0:T(8,128)(2,1)}, bf16[2,1024,128]{1,2,0:T(8,128)(2,1)}, u32[]{:S(2)}, u32[]{:S(2)}) collective-permute-start(bf16[2,1024,128]{1,2,0:T(8,128)(2,1)} %pad_maximum_fusion), channel_id=1, source_target_pairs={{0,16},{16,32},{32,48},{48,64},{64,80},{80,96},{96,112},{1,17},{17... | collective-permute-start | bytes 1572872 | tf_op jit(solution)/shard_map/ppermute | solution.py:19
  109.4 1.5 copy-start.1
  113.4 9.8 %collective-permute-start.14 = (bf16[16,5376]{1,0:T(8,128)(2,1)S(1)}, bf16[16,5376]{1,0:T(8,128)(2,1)S(1)}, u32[]{:S(2)}, u32[]{:S(2)}) collective-permute-start(bf16[16,5376]{1,0:T(8,128)(2,1)S(1)} %slice.122), channel_id=1, source_target_pairs={{0,32},{32,64},{64,96},{96,0},{1,33},{33,65},{65,97},{97,1},{2,34}... | collective-permute-start | bytes 516104 | tf_op jit(solution)/shard_map/ppermute | solution.py:25
  114.4 8.8 %collective-permute-start.15 = (bf16[16,5376]{1,0:T(8,128)(2,1)S(1)}, bf16[16,5376]{1,0:T(8,128)(2,1)S(1)}, u32[]{:S(2)}, u32[]{:S(2)}) collective-permute-start(bf16[16,5376]{1,0:T(8,128)(2,1)S(1)} %slice.123), channel_id=1, source_target_pairs={{0,96},{32,0},{64,32},{96,64},{1,97},{33,1},{65,33},{97,65},{2,98}... | collective-permute-start | bytes 516104 | tf_op jit(solution)/shard_map/ppermute | solution.py:25
  117.7 17.7 %collective-permute-start.12 = (bf16[32,5376]{1,0:T(8,128)(2,1)}, bf16[32,5376]{1,0:T(8,128)(2,1)S(1)}, u32[]{:S(2)}, u32[]{:S(2)}) collective-permute-start(bf16[32,5376]{1,0:T(8,128)(2,1)} %collective-permute-done.10), channel_id=1, source_target_pairs={{0,96},{32,0},{64,32},{96,64},{1,97},{33,1},{65,33},{97,65},{2,98}... | collective-permute-start | bytes 1032200 | tf_op jit(solution)/shard_map/ppermute | solution.py:25
  118.3 15.9 %collective-permute-start.16 = (bf16[32,5376]{1,0:T(8,128)(2,1)}, bf16[32,5376]{1,0:T(8,128)(2,1)S(1)}, u32[]{:S(2)}, u32[]{:S(2)}) collective-permute-start(bf16[32,5376]{1,0:T(8,128)(2,1)} %collective-permute-done.10), channel_id=1, source_target_pairs={{0,32},{32,64},{64,96},{96,0},{1,33},{33,65},{65,97},{97,1},{2,34}... | collective-permute-start | bytes 1032200 | tf_op jit(solution)/shard_map/ppermute | solution.py:25
  122.9 0.9 copy-start.3
  134.2 6.7 %collective-permute-start.17 = (bf16[16,5376]{1,0:T(8,128)(2,1)S(1)}, bf16[16,5376]{1,0:T(8,128)(2,1)S(1)}, u32[]{:S(2)}, u32[]{:S(2)}) collective-permute-start(bf16[16,5376]{1,0:T(8,128)(2,1)S(1)} %slice.124), channel_id=1, source_target_pairs={{0,32},{32,64},{64,96},{96,0},{1,33},{33,65},{65,97},{97,1},{2,34}... | collective-permute-start | bytes 516104 | tf_op jit(solution)/shard_map/ppermute | solution.py:25
  135.5 5.7 %collective-permute-start.18 = (bf16[16,5376]{1,0:T(8,128)(2,1)S(1)}, bf16[16,5376]{1,0:T(8,128)(2,1)S(1)}, u32[]{:S(2)}, u32[]{:S(2)}) collective-permute-start(bf16[16,5376]{1,0:T(8,128)(2,1)S(1)} %slice.125), channel_id=1, source_target_pairs={{0,96},{32,0},{64,32},{96,64},{1,97},{33,1},{65,33},{97,65},{2,98}... | collective-permute-start | bytes 516104 | tf_op jit(solution)/shard_map/ppermute | solution.py:25
  147.2 84.4 %copy-start = (bf16[64,5376]{1,0:T(8,128)(2,1)S(1)}, bf16[64,5376]{1,0:T(8,128)(2,1)}, u32[]{:S(2)}) copy-start(bf16[64,5376]{1,0:T(8,128)(2,1)} %param.9) | copy-start | bytes 2064388
  147.2 84.4 %copy-start.7 = (f32[5376]{0:T(1024)S(1)}, f32[5376]{0:T(1024)}, u32[]{:S(2)}) copy-start(f32[5376]{0:T(1024)} %param.17) | copy-start | bytes 64516
Sparse Core Ops, SparseCore 0:
  10.3 74.6 all-gather.1
  147.4 82.8 reduce-scatter.1
where the time goes:
time: 241 us
  waiting for transfers between devices  126 us (52%)
  starting transfers between devices  33.8 us (14%)
  local copies, waits for them, and re-layouts  24.7 us (10%)
  matrix products  22.8 us (9%)
  other arithmetic  19.8 us (8%)
  between operations  14 us (6%)
    reduce_scatter x1, waiting for transfers between devices, body(): lax.psum_scatter(partial_value, HEAD, scatter_dimension=0, tiled=True)  83 us
    ppermute x18, waiting for transfers between devices, rotated(): return lax.ppermute(shard, axis, pairs)  30.2 us
    ppermute x18, starting transfers between devices, rotated(): return lax.ppermute(shard, axis, pairs)  29.3 us
    dynamic_update_slice x20, local copies, waits for them, and re-layouts, placed(): lax.dynamic_update_index_in_dim(stacked, part, (me + i) % count, 0)  12.8 us
    all_gather x1, waiting for transfers between devices, body(): normed = lax.all_gather(own_normed, HEAD, axis=0, tiled=True)  12.5 us
    dot_general x1, matrix products, body(): projected = jnp.dot(normed, w_in, preferred_element_type=jnp.float32)  10.3 us
    dot_general x1, matrix products, body(): jnp.dot(attended, out_weight, preferred_element_type=jnp.float32)  5.86 us
  transfers between devices with their start and end apart: 21, of which 10 were waited for; matrix products, arithmetic and copies ran while one was open for 17% of the time, Pallas kernels for 0%

commit v1 on v0

--- a/solution.py
+++ b/solution.py
@@ -1,3 +1,4 @@
+import functools
 import jax
 import jax.numpy as jnp
 from jax import lax
@@ -11,6 +12,22 @@
 mask_value = -1e30
 CTX = ("cx", "cy")
 HEAD = ("hc", "core")
+
+
+def turn_bands_on(target, axis_id):
+    big = jnp.concatenate(
+        lax.all_to_all(
+            jnp.stack(lax.axis_size(axis_id) * [target]),
+            split_axis=0,
+            concat_axis=0,
+            axis_name=axis_id,
+        ),
+        axis=0,
+    )
+    return big
+
+
+_process_entries = functools.partial(turn_bands_on, axis_id=HEAD)
 
 
 def passed_along(shard, axis, by):
@@ -91,7 +108,7 @@
     k_cols = w_key.shape[1]
     w_in = gathered_over_ctx(jnp.concatenate([w_query, w_key, value_weight], axis=1))
     own_normed = root_mean_scale(own_rows, pre_gain).astype(jnp.bfloat16)
-    normed = lax.all_gather(own_normed, HEAD, axis=0, tiled=True)
+    normed = _process_entries(own_normed)
     normed, w_output = lax.optimization_barrier((normed, w_output))
     out_weight = gathered_over_ctx(w_output)
     tok_count = normed.shape[0]

time: 241 us -> 392 us (1.63)
  waiting for transfers between devices: 126 us -> 265 us
  starting transfers between devices: 33.8 us -> 41.9 us
  local copies, waits for them, and re-layouts: 24.7 us -> 29.4 us
    ppermute x18, waiting for transfers between devices: 30.2 us -> 184 us  [rotated(): return lax.ppermute(shard, axis, pairs)]
    all_gather x1 -> x0, waiting for transfers between devices: 12.5 us -> none  [body(): normed = lax.all_gather(own_normed, HEAD, axis=0, tiled=True)]
    all_to_all x0 -> x1, starting transfers between devices: none -> 6.72 us  [turn_bands_on(): lax.all_to_all(jnp.stack(lax.axis_size(axis_id) * [target]), split_axis=0...]
    another operation x0 -> x1, local copies, waits for them, and re-layouts: none -> 5.09 us  [turn_bands_on(): jnp.stack(lax.axis_size(axis_id) * [target])]
  transfers between devices with their start and end apart: 21 -> 21, of which waited for: 10 -> 6; matrix products, arithmetic and copies ran while one was open for 17% -> 11% of each run, Pallas kernels for 0% -> 0%
where the time goes in v1:
time: 392 us
  waiting for transfers between devices  265 us (68%)
  starting transfers between devices  41.9 us (11%)
  local copies, waits for them, and re-layouts  29.4 us (8%)
  matrix products  22.8 us (6%)
  other arithmetic  18.9 us (5%)
  between operations  14 us (4%)
    ppermute x18, waiting for transfers between devices, rotated(): return lax.ppermute(shard, axis, pairs)  184 us
    reduce_scatter x1, waiting for transfers between devices, body(): lax.psum_scatter(partial_value, HEAD, scatter_dimension=0, tiled=True)  80.3 us
    ppermute x18, starting transfers between devices, rotated(): return lax.ppermute(shard, axis, pairs)  29.6 us
    dynamic_update_slice x20, local copies, waits for them, and re-layouts, placed(): lax.dynamic_update_index_in_dim(stacked, part, (me + i) % count, 0)  12.8 us
    dot_general x1, matrix products, body(): projected = jnp.dot(normed, w_in, preferred_element_type=jnp.float32)  10.3 us
  transfers between devices with their start and end apart: 21, of which 6 were waited for; matrix products, arithmetic and copies ran while one was open for 11% of the time, Pallas kernels for 0%

profile of v1, /device:TPU:0, one launch (start us, length us, event | category | flops | bytes accessed | tf_op | source)
XLA Modules:
  0.0 391.6 jit_solution(7319361529158923659)
XLA Ops:
  6.5 1.3 fusion.10
  7.9 1.3 fusion.12
  9.2 5.1 %stack.6 = bf16[16,64,5376]{2,1,0:T(8,128)(2,1)} broadcast(bf16[64,5376]{1,0:T(8,128)(2,1)S(1)} %fusion.12), dimensions={1,2} | broadcast | bytes 11698176 | tf_op jit(solution)/shard_map/stack | solution.py:20
  14.3 6.7 %all-to-all-start = ((bf16[16,64,5376]{2,1,0:T(8,128)(2,1)}), bf16[16,64,5376]{2,1,0:T(8,128)(2,1)}, u32[]{:S(2)}, u32[]{:S(2)}) async-start(bf16[16,64,5376]{2,1,0:T(8,128)(2,1)} %stack.6), calls=%async_computation | async-start | bytes 22020096 | tf_op jit(solution)/shard_map/all_to_all | solution.py:19
  21.1 0.8 constant_dynamic-update-slice_fusion.2
  21.9 0.7 constant_dynamic-update-slice_fusion.1
  22.5 0.7 constant_dynamic-update-slice_fusion
  23.2 2.9 collective-permute-start
  26.1 2.8 collective-permute-start.1
  29.0 0.1 broadcast_in_dim.113.clone
  29.1 1.2 bitcast_dynamic-update-slice_fusion.5
  30.2 1.1 and_and_fusion.1
  31.4 2.9 multiply_cosine_fusion
  34.3 1.1 and_and_fusion
  35.4 12.0 %collective-permute-done.3 = bf16[672,512]{1,0:T(8,128)(2,1)S(1)} collective-permute-done((bf16[672,512]{1,0:T(8,128)(2,1)}, bf16[672,512]{1,0:T(8,128)(2,1)S(1)}, u32[]{:S(2)}, u32[]{:S(2)}) %collective-permute-start.3) | collective-permute-done | bytes 688160 | tf_op jit(solution)/shard_map/ppermute | solution.py:42
  47.6 1.0 slice.106
  48.6 3.3 collective-permute-start.5
  51.9 152.7 %collective-permute-done = bf16[672,512]{1,0:T(8,128)(2,1)} collective-permute-done((bf16[672,512]{1,0:T(8,128)(2,1)}, bf16[672,512]{1,0:T(8,128)(2,1)}, u32[]{:S(2)}, u32[]{:S(2)}) %collective-permute-start) | collective-permute-done | bytes 688160 | tf_op jit(solution)/shard_map/ppermute | solution.py:42
  204.5 2.8 collective-permute-start.2
  207.4 1.2 bitcast_dynamic-update-slice_fusion.3
  208.6 1.2 bitcast_dynamic-update-slice_fusion.4
  209.7 2.9 broadcast_in_dim.112
  212.6 1.2 constant_dynamic-update-slice_fusion.10
  214.2 11.5 %collective-permute-done.6 = bf16[672,512]{1,0:T(8,128)(2,1)S(1)} collective-permute-done((bf16[672,512]{1,0:T(8,128)(2,1)}, bf16[672,512]{1,0:T(8,128)(2,1)S(1)}, u32[]{:S(2)}, u32[]{:S(2)}) %collective-permute-start.6) | collective-permute-done | bytes 688160 | tf_op jit(solution)/shard_map/ppermute | solution.py:42
  225.9 3.5 collective-permute-start.8
  229.4 1.2 constant_dynamic-update-slice_fusion.9
  230.6 5.2 %collective-permute-done.7 = bf16[336,512]{1,0:T(8,128)(2,1)S(1)} collective-permute-done((bf16[336,512]{1,0:T(8,128)(2,1)S(1)}, bf16[336,512]{1,0:T(8,128)(2,1)S(1)}, u32[]{:S(2)}, u32[]{:S(2)}) %collective-permute-start.7) | collective-permute-done | bytes 344096 | tf_op jit(solution)/shard_map/ppermute | solution.py:42
  235.8 1.3 constant_dynamic-update-slice_fusion.8
  237.1 1.2 constant_dynamic-update-slice_fusion.7
  238.3 10.3 %fusion.48 = f32[1024,512]{0,1:T(8,128)S(1)} fusion(bf16[1024,5376]{1,0:T(8,128)(2,1)} %bitcast, bf16[5376,512]{1,0:T(8,128)(2,1)} %bitcast.9), kind=kOutput, calls=%fused_computation.115 | convolution fusion | flops 5637144576 | bytes 18612224 | tf_op jit(solution)/shard_map/dot_general | solution.py:115
  248.8 1.1 slice.115
  249.8 0.1 multiply_reduce_fusion
  250.0 3.3 collective-permute-start.11
  253.3 0.6 collective-permute-start.10
  253.9 0.1 multiply_bitcast_fusion
  254.1 1.2 fusion.42
  255.2 0.8 pad_maximum_fusion
  256.1 5.6 %collective-permute-start.9 = (bf16[2,1024,128]{1,2,0:T(8,128)(2,1)}, bf16[2,1024,128]{1,2,0:T(8,128)(2,1)}, u32[]{:S(2)}, u32[]{:S(2)}) collective-permute-start(bf16[2,1024,128]{1,2,0:T(8,128)(2,1)} %pad_maximum_fusion), channel_id=1, source_target_pairs={{0,16},{16,32},{32,48},{48,64},{64,80},{80,96},{96,112},{1,17},{17... | collective-permute-start | bytes 1572872 | tf_op jit(solution)/shard_map/ppermute | solution.py:36
  261.7 1.5 copy.10
  263.3 1.1 bitcast_dynamic-update-slice_fusion.11
  264.4 0.3 multiply_multiply_fusion
  264.8 0.5 multiply_subtract_fusion
  265.3 0.3 fusion.20
  265.6 0.9 slice.122
  266.7 0.9 slice.123
  267.6 3.3 collective-permute-start.15
  270.9 1.0 bitcast_dynamic-update-slice_fusion.10
  271.9 0.2 broadcast_in_dim.125
  272.2 3.2 collective-permute-start.12
  275.5 1.0 bitcast_dynamic-update-slice_fusion.9
  276.6 1.0 bitcast_dynamic-update-slice_fusion.7
  277.7 1.1 maximum_maximum_fusion
  278.8 1.3 fusion
  280.1 1.3 fusion.2
  281.4 2.0 fusion.14
  283.5 1.3 fusion.1
  284.7 1.3 fusion.3
  286.1 2.0 fusion.17
  288.2 3.5 collective-permute-start.18
  291.9 2.9 collective-permute-done.17
  295.0 5.9 %convolution_convert_fusion = bf16[1024,5376]{1,0:T(8,128)(2,1)} fusion(bf16[256,5376]{1,0:T(8,128)(2,1)S(1)} %bitcast.132, bf16[512,256]{0,1:T(8,128)(2,1)S(1)} %bitcast.135, bf16[512,256]{0,1:T(8,128)(2,1)S(1)} %bitcast.134), kind=kOutput, calls=%fused_computation | convolution fusion | flops 2825125888 | bytes 14286848 | tf_op jit(solution)/shard_map/dot_general | solution.py:176
  300.9 80.3 %reduce-scatter.2.cloned.1.call-done = bf16[64,5376]{1,0:T(8,128)(2,1)} async-done(((bf16[1024,5376]{1,0:T(8,128)(2,1)}), bf16[64,5376]{1,0:T(8,128)(2,1)}) %reduce-scatter.2.cloned.1.call-update) | async-done | bytes 688144 | tf_op jit(solution)/shard_map/reduce_scatter | solution.py:179
  381.1 1.3 fusion.8
  382.5 2.3 fusion.13
  (82 shorter events, 1.9 us)
Async XLA Ops:
  14.3 6.8 %copy-start.4 = (bf16[672,256]{1,0:T(8,128)(2,1)S(1)}, bf16[672,256]{1,0:T(8,128)(2,1)}, u32[]{:S(2)}) copy-start(bf16[672,256]{1,0:T(8,128)(2,1)} %param.11) | copy-start | bytes 1032196
  14.3 7.5 %copy-start.5 = (bf16[672,128]{1,0:T(8,128)(2,1)S(1)}, bf16[672,128]{1,0:T(8,128)(2,1)}, u32[]{:S(2)}) copy-start(bf16[672,128]{1,0:T(8,128)(2,1)} %param.12) | copy-start | bytes 516100
  14.3 8.2 %copy-start.6 = (bf16[672,128]{1,0:T(8,128)(2,1)S(1)}, bf16[672,128]{1,0:T(8,128)(2,1)}, u32[]{:S(2)}) copy-start(bf16[672,128]{1,0:T(8,128)(2,1)} %param.13) | copy-start | bytes 516100
  14.3 224.0 %all-to-all-start = ((bf16[16,64,5376]{2,1,0:T(8,128)(2,1)}), bf16[16,64,5376]{2,1,0:T(8,128)(2,1)}, u32[]{:S(2)}, u32[]{:S(2)}) async-start(bf16[16,64,5376]{2,1,0:T(8,128)(2,1)} %stack.6), calls=%async_computation | async-start | bytes 22020096 | tf_op jit(solution)/shard_map/all_to_all | solution.py:19
  21.0 360.1 %reduce-scatter.2.cloned.1.call-start = ((), (), s32[]{:S(2)}) async-start(), calls=%async_computation.2 | async-start | bytes 11698176 | tf_op jit(solution)/shard_map/reduce_scatter | solution.py:179
  23.2 181.3 %collective-permute-start = (bf16[672,512]{1,0:T(8,128)(2,1)}, bf16[672,512]{1,0:T(8,128)(2,1)}, u32[]{:S(2)}, u32[]{:S(2)}) collective-permute-start(bf16[672,512]{1,0:T(8,128)(2,1)} %constant_dynamic-update-slice_fusion), channel_id=1, source_target_pairs={{0,16},{16,0},{1,17},{17,1},{2,18},{18,2},{3,19},{19,3},{4,20},{20... | collective-permute-start | bytes 2064392 | tf_op jit(solution)/shard_map/ppermute | solution.py:42
  26.1 21.4 %collective-permute-start.1 = (bf16[672,512]{1,0:T(8,128)(2,1)}, bf16[672,512]{1,0:T(8,128)(2,1)}, u32[]{:S(2)}, u32[]{:S(2)}) collective-permute-start(bf16[672,512]{1,0:T(8,128)(2,1)} %constant_dynamic-update-slice_fusion), channel_id=1, source_target_pairs={{0,96},{32,0},{64,32},{96,64},{1,97},{33,1},{65,33},{97,65},{2,98}... | collective-permute-start | bytes 2064392 | tf_op jit(solution)/shard_map/ppermute | solution.py:42
  28.9 18.6 %collective-permute-start.3 = (bf16[672,512]{1,0:T(8,128)(2,1)}, bf16[672,512]{1,0:T(8,128)(2,1)S(1)}, u32[]{:S(2)}, u32[]{:S(2)}) collective-permute-start(bf16[672,512]{1,0:T(8,128)(2,1)} %constant_dynamic-update-slice_fusion), channel_id=1, source_target_pairs={{0,32},{32,64},{64,96},{96,0},{1,33},{33,65},{65,97},{97,1},{2,34}... | collective-permute-start | bytes 2064392 | tf_op jit(solution)/shard_map/ppermute | solution.py:42
  47.5 166.5 %collective-permute-start.4 = (bf16[336,512]{1,0:T(8,128)(2,1)S(1)}, bf16[336,512]{1,0:T(8,128)(2,1)S(1)}, u32[]{:S(2)}, u32[]{:S(2)}) collective-permute-start(bf16[336,512]{1,0:T(8,128)(2,1)S(1)} %slice.105), channel_id=1, source_target_pairs={{0,32},{32,64},{64,96},{96,0},{1,33},{33,65},{65,97},{97,1},{2,34}... | collective-permute-start | bytes 1032200 | tf_op jit(solution)/shard_map/ppermute | solution.py:42
  48.6 165.4 %collective-permute-start.5 = (bf16[336,512]{1,0:T(8,128)(2,1)S(1)}, bf16[336,512]{1,0:T(8,128)(2,1)S(1)}, u32[]{:S(2)}, u32[]{:S(2)}) collective-permute-start(bf16[336,512]{1,0:T(8,128)(2,1)S(1)} %slice.106), channel_id=1, source_target_pairs={{0,96},{32,0},{64,32},{96,64},{1,97},{33,1},{65,33},{97,65},{2,98}... | collective-permute-start | bytes 1032200 | tf_op jit(solution)/shard_map/ppermute | solution.py:42
  204.5 21.3 %collective-permute-start.2 = (bf16[672,512]{1,0:T(8,128)(2,1)}, bf16[672,512]{1,0:T(8,128)(2,1)S(1)}, u32[]{:S(2)}, u32[]{:S(2)}) collective-permute-start(bf16[672,512]{1,0:T(8,128)(2,1)} %collective-permute-done), channel_id=1, source_target_pairs={{0,96},{32,0},{64,32},{96,64},{1,97},{33,1},{65,33},{97,65},{2,98}... | collective-permute-start | bytes 2064392 | tf_op jit(solution)/shard_map/ppermute | solution.py:42
  207.3 18.4 %collective-permute-start.6 = (bf16[672,512]{1,0:T(8,128)(2,1)}, bf16[672,512]{1,0:T(8,128)(2,1)S(1)}, u32[]{:S(2)}, u32[]{:S(2)}) collective-permute-start(bf16[672,512]{1,0:T(8,128)(2,1)} %collective-permute-done), channel_id=1, source_target_pairs={{0,32},{32,64},{64,96},{96,0},{1,33},{33,65},{65,97},{97,1},{2,34}... | collective-permute-start | bytes 2064392 | tf_op jit(solution)/shard_map/ppermute | solution.py:42
  225.7 10.0 %collective-permute-start.7 = (bf16[336,512]{1,0:T(8,128)(2,1)S(1)}, bf16[336,512]{1,0:T(8,128)(2,1)S(1)}, u32[]{:S(2)}, u32[]{:S(2)}) collective-permute-start(bf16[336,512]{1,0:T(8,128)(2,1)S(1)} %slice.107), channel_id=1, source_target_pairs={{0,32},{32,64},{64,96},{96,0},{1,33},{33,65},{65,97},{97,1},{2,34}... | collective-permute-start | bytes 1032200 | tf_op jit(solution)/shard_map/ppermute | solution.py:42
  225.9 9.9 %collective-permute-start.8 = (bf16[336,512]{1,0:T(8,128)(2,1)S(1)}, bf16[336,512]{1,0:T(8,128)(2,1)S(1)}, u32[]{:S(2)}, u32[]{:S(2)}) collective-permute-start(bf16[336,512]{1,0:T(8,128)(2,1)S(1)} %slice.108), channel_id=1, source_target_pairs={{0,96},{32,0},{64,32},{96,64},{1,97},{33,1},{65,33},{97,65},{2,98}... | collective-permute-start | bytes 1032200 | tf_op jit(solution)/shard_map/ppermute | solution.py:42
  248.6 5.3 %copy-start.8 = (f32[128]{0:T(128)S(1)}, f32[128]{0:T(128)}, u32[]{:S(2)}) copy-start(f32[128]{0:T(128)} %param.15) | copy-start | bytes 1540
  249.9 15.7 %collective-permute-start.13 = (bf16[32,5376]{1,0:T(8,128)(2,1)}, bf16[32,5376]{1,0:T(8,128)(2,1)}, u32[]{:S(2)}, u32[]{:S(2)}) collective-permute-start(bf16[32,5376]{1,0:T(8,128)(2,1)} %param.16), channel_id=1, source_target_pairs={{0,32},{32,64},{64,96},{96,0},{1,33},{33,65},{65,97},{97,1},{2,34}... | collective-permute-start | bytes 1032200 | tf_op jit(solution)/shard_map/ppermute | solution.py:42
  250.0 16.6 %collective-permute-start.11 = (bf16[32,5376]{1,0:T(8,128)(2,1)}, bf16[32,5376]{1,0:T(8,128)(2,1)}, u32[]{:S(2)}, u32[]{:S(2)}) collective-permute-start(bf16[32,5376]{1,0:T(8,128)(2,1)} %param.16), channel_id=1, source_target_pairs={{0,96},{32,0},{64,32},{96,64},{1,97},{33,1},{65,33},{97,65},{2,98}... | collective-permute-start | bytes 1032200 | tf_op jit(solution)/shard_map/ppermute | solution.py:42
  253.3 17.6 %collective-permute-start.10 = (bf16[32,5376]{1,0:T(8,128)(2,1)}, bf16[32,5376]{1,0:T(8,128)(2,1)}, u32[]{:S(2)}, u32[]{:S(2)}) collective-permute-start(bf16[32,5376]{1,0:T(8,128)(2,1)} %param.16), channel_id=1, source_target_pairs={{0,16},{16,0},{1,17},{17,1},{2,18},{18,2},{3,19},{19,3},{4,20},{20... | collective-permute-start | bytes 1032200 | tf_op jit(solution)/shard_map/ppermute | solution.py:42
  254.0 10.4 %copy-start.9 = (f32[128]{0:T(128)S(1)}, f32[128]{0:T(128)}, u32[]{:S(2)}) copy-start(f32[128]{0:T(128)} %param.14) | copy-start | bytes 1540
  255.2 6.5 %copy-start.2 = (bf16[1,1024,64]{1,2,0:T(8,128)(2,1)}, bf16[1,1024,64]{1,2,0:T(8,128)(2,1)S(1)}, u32[]{:S(2)}) copy-start(bf16[1,1024,64]{1,2,0:T(8,128)(2,1)S(1)} %get-tuple-element.12) | copy-start | bytes 393220
  256.1 21.6 %collective-permute-start.9 = (bf16[2,1024,128]{1,2,0:T(8,128)(2,1)}, bf16[2,1024,128]{1,2,0:T(8,128)(2,1)}, u32[]{:S(2)}, u32[]{:S(2)}) collective-permute-start(bf16[2,1024,128]{1,2,0:T(8,128)(2,1)} %pad_maximum_fusion), channel_id=1, source_target_pairs={{0,16},{16,32},{32,48},{48,64},{64,80},{80,96},{96,112},{1,17},{17... | collective-permute-start | bytes 1572872 | tf_op jit(solution)/shard_map/ppermute | solution.py:36
  263.3 1.5 copy-start.1
  266.6 11.0 %collective-permute-start.14 = (bf16[16,5376]{1,0:T(8,128)(2,1)S(1)}, bf16[16,5376]{1,0:T(8,128)(2,1)S(1)}, u32[]{:S(2)}, u32[]{:S(2)}) collective-permute-start(bf16[16,5376]{1,0:T(8,128)(2,1)S(1)} %slice.122), channel_id=1, source_target_pairs={{0,32},{32,64},{64,96},{96,0},{1,33},{33,65},{65,97},{97,1},{2,34}... | collective-permute-start | bytes 516104 | tf_op jit(solution)/shard_map/ppermute | solution.py:42
  267.6 10.0 %collective-permute-start.15 = (bf16[16,5376]{1,0:T(8,128)(2,1)S(1)}, bf16[16,5376]{1,0:T(8,128)(2,1)S(1)}, u32[]{:S(2)}, u32[]{:S(2)}) collective-permute-start(bf16[16,5376]{1,0:T(8,128)(2,1)S(1)} %slice.123), channel_id=1, source_target_pairs={{0,96},{32,0},{64,32},{96,64},{1,97},{33,1},{65,33},{97,65},{2,98}... | collective-permute-start | bytes 516104 | tf_op jit(solution)/shard_map/ppermute | solution.py:42
  272.1 5.6 %copy-start.3 = (bf16[1,1024,64]{1,2,0:T(8,128)(2,1)S(1)}, bf16[1,1024,64]{1,2,0:T(8,128)(2,1)}, u32[]{:S(2)}) copy-start(bf16[1,1024,64]{1,2,0:T(8,128)(2,1)} %copy-done.2) | copy-start | bytes 393220
  272.1 16.0 %collective-permute-start.16 = (bf16[32,5376]{1,0:T(8,128)(2,1)}, bf16[32,5376]{1,0:T(8,128)(2,1)S(1)}, u32[]{:S(2)}, u32[]{:S(2)}) collective-permute-start(bf16[32,5376]{1,0:T(8,128)(2,1)} %collective-permute-done.10), channel_id=1, source_target_pairs={{0,32},{32,64},{64,96},{96,0},{1,33},{33,65},{65,97},{97,1},{2,34}... | collective-permute-start | bytes 1032200 | tf_op jit(solution)/shard_map/ppermute | solution.py:42
  272.2 16.0 %collective-permute-start.12 = (bf16[32,5376]{1,0:T(8,128)(2,1)}, bf16[32,5376]{1,0:T(8,128)(2,1)S(1)}, u32[]{:S(2)}, u32[]{:S(2)}) collective-permute-start(bf16[32,5376]{1,0:T(8,128)(2,1)} %collective-permute-done.10), channel_id=1, source_target_pairs={{0,96},{32,0},{64,32},{96,64},{1,97},{33,1},{65,33},{97,65},{2,98}... | collective-permute-start | bytes 1032200 | tf_op jit(solution)/shard_map/ppermute | solution.py:42
  288.1 6.7 %collective-permute-start.17 = (bf16[16,5376]{1,0:T(8,128)(2,1)S(1)}, bf16[16,5376]{1,0:T(8,128)(2,1)S(1)}, u32[]{:S(2)}, u32[]{:S(2)}) collective-permute-start(bf16[16,5376]{1,0:T(8,128)(2,1)S(1)} %slice.124), channel_id=1, source_target_pairs={{0,32},{32,64},{64,96},{96,0},{1,33},{33,65},{65,97},{97,1},{2,34}... | collective-permute-start | bytes 516104 | tf_op jit(solution)/shard_map/ppermute | solution.py:42
  288.2 6.6 %collective-permute-start.18 = (bf16[16,5376]{1,0:T(8,128)(2,1)S(1)}, bf16[16,5376]{1,0:T(8,128)(2,1)S(1)}, u32[]{:S(2)}, u32[]{:S(2)}) collective-permute-start(bf16[16,5376]{1,0:T(8,128)(2,1)S(1)} %slice.125), channel_id=1, source_target_pairs={{0,96},{32,0},{64,32},{96,64},{1,97},{33,1},{65,33},{97,65},{2,98}... | collective-permute-start | bytes 516104 | tf_op jit(solution)/shard_map/ppermute | solution.py:42
  300.8 81.6 %copy-start = (bf16[64,5376]{1,0:T(8,128)(2,1)S(1)}, bf16[64,5376]{1,0:T(8,128)(2,1)}, u32[]{:S(2)}) copy-start(bf16[64,5376]{1,0:T(8,128)(2,1)} %param.9) | copy-start | bytes 2064388
  300.8 81.6 %copy-start.7 = (f32[5376]{0:T(1024)S(1)}, f32[5376]{0:T(1024)}, u32[]{:S(2)}) copy-start(f32[5376]{0:T(1024)} %param.17) | copy-start | bytes 64516
Sparse Core Ops, SparseCore 0:
  301.0 80.0 reduce-scatter.1
